TPU v7x, 256 devices: a whole 4x4x8 slice. The times are simulated.
256 devices in a mesh: gy: 8 (over y, x_hi), gx: 4 (over x_lo, core), wa: 8 (over z).
Axes of the slice: x: 4 (x_hi: 2, x_lo: 2; x = x_hi * 2 + x_lo), y: 4, z: 8, core: 2. Of those that a mesh axis runs over, the one named last changes fastest.
Arguments:
- tokens: bfloat16 [8, 64, 128, 3072], P('wa', 'gy', 'gx'), may hold values from -6 to 6
- mod_shift: float32 [8, 3072], P('wa'), may hold values from -3 to 3
- mod_scale: float32 [8, 3072], P('wa'), may hold values from -0.9 to 3.9
- qkv_weight: bfloat16 [3072, 4608], P(None, ('gx', 'wa')), may hold values from -0.14433757 to 0.14433757
- block_codes: int32 [8, 16, 9], P('gy', 'gx'), may hold values from 0 to 8, as said below
- block_counts: int32 [8, 16], P('gy', 'gx'), may hold values from 1 to 9, as said below
- valid_tokens: int32 [8, 16], replicated, may hold values from 1 to 64
Outputs:
- attended: bfloat16 [8, 64, 128, 1536], P('wa', 'gy', 'gx')
Inputs may be any that keep to these rules, and one draw needn't show every extreme that they name: `block_codes`: the 9 codes of a block's list are distinct, the first is 4 (the block itself), and the first block_counts entries name blocks inside the grid. `block_counts`: A count never exceeds the number of blocks of the 3 x 3 neighbourhood that lie inside the grid.
All inputs are finite; a program needn't handle non-finite values.
Results may differ from a plain program's by a relative error of at most 0.007.
Values may be sent and summed in bfloat16 or wider, within the bound.
No kernel may reach another device: no remote copies, remote signals or barrier semaphores. Data moves between devices by JAX's collectives and lax.ppermute only.
A program may use at most 128 MiB of HBM per device.

v0:
```python
import math
import jax
import jax.numpy as jnp
from jax import lax
from jax.sharding import PartitionSpec as P

D = 3072
HEADS = 12
HD = 128
BLK = 8
NBR = 9


def extended_2(array, sides, width):
    for axis, dim in sides:
        size, length = (lax.axis_size(axis), array.shape[dim])
        up = [(i, (i + 1) % size) for i in range(size - 1)]
        down = [(j, i) for i, j in up]
        last = lax.slice_in_dim(array, length - width, length, axis=dim)
        first = lax.slice_in_dim(array, 0, width, axis=dim)
        before = lax.ppermute(last, axis, up)
        after = lax.ppermute(first, axis, down)
        array = jnp.concatenate([before, array, after], axis=dim)
    return array


def normalize(rows, shift_row, scale_row):
    widened = rows.astype(jnp.float32)
    average = jnp.mean(widened, axis=-1, keepdims=True)
    centred = widened - average
    spread = jnp.mean(centred * centred, axis=-1, keepdims=True)
    return (centred * lax.rsqrt(spread + 1e-06) * (1.0 + scale_row) + shift_row).astype(
        jnp.bfloat16
    )


def to_blocks(field):
    height, breadth, channels = field.shape
    shaped = field.reshape(height // BLK, BLK, breadth // BLK, BLK, channels)
    return shaped.transpose(0, 2, 1, 3, 4).reshape(
        height // BLK, breadth // BLK, BLK * BLK, channels
    )


def from_blocks(blocks):
    block_rows, block_cols, cells, channels = blocks.shape
    shaped = blocks.reshape(block_rows, block_cols, BLK, BLK, channels)
    return shaped.transpose(0, 2, 1, 3, 4).reshape(block_rows * BLK, block_cols * BLK, channels)


def make_mask(counts, live_count):
    slot_ids = jnp.arange(NBR, dtype=jnp.int32)
    token_ids = jnp.arange(BLK * BLK, dtype=jnp.int32)
    used = slot_ids[:, None] < counts[..., None, None]
    return used & (token_ids < live_count[..., None])


def attend(queries, key_blocks, key_mask):
    number = queries.shape[0]
    query_heads = queries.reshape(number, BLK * BLK, HEADS, HD)
    key_value = key_blocks.reshape(number, NBR * BLK * BLK, 2, HEADS, HD)
    scores = jnp.einsum(
        "nqhd,nkhd->nhqk", query_heads, key_value[:, :, 0], preferred_element_type=jnp.float32
    ) * (1.0 / math.sqrt(HD))
    scores = jnp.where(key_mask[:, None, None, :], scores, -jnp.inf)
    highest = jnp.max(scores, axis=-1, keepdims=True)
    exponent = jnp.exp(scores - highest)
    probs = (exponent / jnp.sum(exponent, axis=-1, keepdims=True)).astype(jnp.bfloat16)
    blended = jnp.einsum(
        "nhqk,nkhd->nqhd", probs, key_value[:, :, 1], preferred_element_type=jnp.float32
    )
    return blended.astype(jnp.bfloat16).reshape(number, BLK * BLK, HEADS * HD)


def body(tokens, mod_shift, mod_scale, qkv_weight, block_codes, block_counts, valid_tokens):
    tile_rows = tokens.shape[1]
    tile_cols = tokens.shape[2]
    width = HEADS * HD
    flat_rows = normalize(tokens[0], mod_shift[0], mod_scale[0]).reshape(tile_rows * tile_cols, D)
    qkv = jnp.dot(
        flat_rows,
        lax.all_gather(qkv_weight, ("gx", "wa"), axis=1, tiled=True),
        preferred_element_type=jnp.float32,
    ).astype(jnp.bfloat16)
    qkv_grid = qkv.reshape(tile_rows, tile_cols, 3 * width)
    extended = extended_2(qkv_grid[:, :, width:], (("gy", 0), ("gx", 1)), BLK)
    block_rows = tile_rows // BLK
    block_cols = tile_cols // BLK
    queries = to_blocks(qkv_grid[:, :, :width])
    key_blocks = to_blocks(extended)
    row_ids = jnp.arange(block_rows, dtype=jnp.int32)[:, None, None]
    col_ids = jnp.arange(block_cols, dtype=jnp.int32)[None, :, None]
    row_step = block_codes // 3 - 1
    col_step = block_codes % 3 - 1
    picked = key_blocks[row_ids + 1 + row_step, col_ids + 1 + col_step]
    global_row = jnp.clip(
        lax.axis_index("gy") * block_rows + row_ids + row_step, 0, valid_tokens.shape[0] - 1
    )
    global_col = jnp.clip(
        lax.axis_index("gx") * block_cols + col_ids + col_step, 0, valid_tokens.shape[1] - 1
    )
    live_count = valid_tokens[global_row, global_col]
    key_mask = make_mask(block_counts, live_count)
    number = block_rows * block_cols
    result = attend(
        queries.reshape(number, BLK * BLK, width),
        picked.reshape(number, NBR, BLK * BLK, 2 * width),
        key_mask.reshape(number, NBR * BLK * BLK),
    )
    return from_blocks(result.reshape(block_rows, block_cols, BLK * BLK, width))[None]


def solution(mesh):
    return jax.shard_map(
        body,
        mesh=mesh,
        in_specs=(
            P("wa", "gy", "gx", None),
            P("wa", None),
            P("wa", None),
            P(None, ("gx", "wa")),
            P("gy", "gx", None),
            P("gy", "gx"),
            P(),
        ),
        out_specs=P("wa", "gy", "gx", None),
        check_vma=False,
    )
```

profile of v0, /device:TPU:29, one launch (start us, length us, event | category | flops | bytes accessed | tf_op | source)
XLA Modules:
  0.0 368.1 jit_solution(4767164489304758296)
XLA Ops:
  6.5 0.0 all-gather.2.cloned.1.call-start
  6.6 0.7 all-gather.2.cloned.1.call-update
  7.3 1.7 convert_reduce_fusion
  9.0 0.1 div.23
  9.1 2.0 fusion.8
  11.0 0.1 rsqrt.12
  11.2 0.8 fusion.12
  12.0 0.0 copy-start.7
  12.0 162.2 %all-gather.2.cloned.1.call-done = bf16[3072,4608]{0,1:T(8,128)(2,1)} async-done(((bf16[3072,144]{0,1:T(8,128)(2,1)}), bf16[3072,4608]{0,1:T(8,128)(2,1)}) %all-gather.2.cloned.1.call-update) | async-done | bytes 28311568 | tf_op jit(solution)/shard_map/all_gather | solution.py:82
  174.2 13.0 %convolution_convert_fusion = bf16[256,4608]{1,0:T(8,128)(2,1)S(1)} fusion(bf16[256,3072]{1,0:T(8,128)(2,1)S(1)} %fusion.12, bf16[3072,4608]{0,1:T(8,128)(2,1)} %all-gather.2.cloned.1.call-done), kind=kOutput, calls=%fused_computation.12 | convolution fusion | flops 7248936960 | bytes 32243712 | tf_op jit(solution)/shard_map/dot_general | solution.py:80
  187.2 0.2 slice.31
  187.4 1.2 copy-done.4
  188.6 2.4 collective-permute-start.1
  191.0 1.3 collective-permute-start
  192.4 0.0 copy-done.7
  192.4 0.1 fusion.19
  192.4 0.0 copy-start.8
  192.5 31.9 %collective-permute-done.1 = bf16[8,32,3072]{2,1,0:T(8,128)(2,1)S(1)} collective-permute-done((bf16[8,32,3072]{2,1,0:T(8,128)(2,1)S(1)}, bf16[8,32,3072]{2,1,0:T(8,128)(2,1)S(1)}, u32[]{:S(2)}, u32[]{:S(2)}) %collective-permute-start.1) | collective-permute-done | bytes 1572896 | tf_op jit(solution)/shard_map/ppermute | solution.py:22
  224.4 37.2 %collective-permute-done = bf16[8,32,3072]{2,1,0:T(8,128)(2,1)} collective-permute-done((bf16[8,32,3072]{2,1,0:T(8,128)(2,1)S(1)}, bf16[8,32,3072]{2,1,0:T(8,128)(2,1)}, u32[]{:S(2)}, u32[]{:S(2)}) %collective-permute-start) | collective-permute-done | bytes 1572896 | tf_op jit(solution)/shard_map/ppermute | solution.py:21
  261.6 2.8 pad_maximum_fusion.3
  264.4 4.1 %collective-permute-start.2 = (bf16[24,8,3072]{2,1,0:T(8,128)(2,1)}, bf16[24,8,3072]{2,1,0:T(8,128)(2,1)}, u32[]{:S(2)}, u32[]{:S(2)}) collective-permute-start(bf16[24,8,3072]{2,1,0:T(8,128)(2,1)} %get-tuple-element.7), channel_id=1, source_target_pairs={{0,8},{8,16},{16,24},{1,9},{9,17},{17,25},{2,10},{10,18},{18,26},{... | collective-permute-start | bytes 3538952 | tf_op jit(solution)/shard_map/ppermute | solution.py:21
  268.5 2.1 collective-permute-start.3
  270.6 0.1 reshape.140
  270.7 0.9 gather_fusion.1
  271.5 0.1 lt.77
  271.6 0.1 reshape.132
  271.7 0.1 iota_compare_fusion
  271.8 0.1 and.28
  271.9 0.1 and.29
  272.0 0.1 lt.73
  272.0 0.1 lt.78
  272.1 0.1 lt.79
  272.2 1.2 slice_bitcast_fusion
  273.4 0.9 copy.14
  274.4 2.4 reshape_reshape_reshape.6
  276.7 5.2 %collective-permute-done.2 = bf16[24,8,3072]{2,1,0:T(8,128)(2,1)} collective-permute-done((bf16[24,8,3072]{2,1,0:T(8,128)(2,1)}, bf16[24,8,3072]{2,1,0:T(8,128)(2,1)}, u32[]{:S(2)}, u32[]{:S(2)}) %collective-permute-start.2) | collective-permute-done | bytes 1179680 | tf_op jit(solution)/shard_map/ppermute | solution.py:21
  281.9 4.4 %collective-permute-done.3 = bf16[24,8,3072]{2,1,0:T(8,128)(2,1)} collective-permute-done((bf16[24,8,3072]{2,1,0:T(8,128)(2,1)}, bf16[24,8,3072]{2,1,0:T(8,128)(2,1)}, u32[]{:S(2)}, u32[]{:S(2)}) %collective-permute-start.3) | collective-permute-done | bytes 1179680 | tf_op jit(solution)/shard_map/ppermute | solution.py:22
  286.3 3.3 pad_maximum_fusion
  289.6 3.7 %copy.33 = bf16[3,6,8,8,3072]{4,3,2,1,0:T(8,128)(2,1)} copy(bf16[3,6,8,8,3072]{4,3,1,2,0:T(8,128)(2,1)S(1)} %bitcast.68) | data formatting | bytes 14155776 | tf_op jit(solution)/shard_map/transpose | solution.py:40
  293.4 10.5 %gather_fusion = bf16[36,64,3072]{2,1,0:T(8,128)(2,1)} fusion(bf16[3,6,64,3072]{3,2,1,0:T(8,128)(2,1)} %bitcast.67, s32[36]{0:T(128)S(1)} %reshape.132), kind=kCustom, calls=%fused_computation | custom fusion | bytes 28311840 | tf_op jit(solution)/shard_map/gather | solution.py:95
  303.9 25.4 %reshape_reshape.3 = bf16[4,576,2,12,128]{4,3,2,1,0:T(8,128)(2,1)} reshape(bf16[36,64,3072]{2,1,0:T(8,128)(2,1)} %gather_fusion) | data formatting | bytes 28311552 | tf_op jit(solution)/shard_map/reshape;reshape | solution.py:61
  329.3 12.5 %fusion.30 = (bf16[4,576,1,12,128]{4,3,2,1,0:T(8,128)(2,1)S(1)}, bf16[4,576,1,12,128]{4,3,2,1,0:T(8,128)(2,1)}) fusion(bf16[4,576,2,12,128]{4,3,2,1,0:T(8,128)(2,1)} %reshape_reshape.3), kind=kLoop, calls=%fused_computation.69 | loop fusion | bytes 28311552 | tf_op jit(solution)/shard_map/slice | solution.py:63
  341.8 3.4 fusion.2
  345.2 4.4 %fusion.31 = (f32[4,12,64]{2,1,0:T(8,128)S(1)}, f32[4,12,64,576]{3,2,1,0:T(8,128)}) fusion(f32[4,12,64,576]{3,2,1,0:T(8,128)S(1)} %fusion.2, pred[4,576]{1,0:T(4,128)(4,1)S(1)} %compare_and_fusion), kind=kOutput, calls=%fused_computation.70 | output fusion | flops 10617407 | bytes 14170368 | tf_op jit(solution)/shard_map/sub | solution.py:67
  349.7 9.6 %fusion.14 = bf16[4,64,12,128]{3,1,2,0:T(8,128)(2,1)S(1)} fusion(bf16[4,576,1,12,128]{4,3,2,1,0:T(8,128)(2,1)} %get-tuple-element.6, f32[4,12,64,576]{3,2,1,0:T(8,128)} %get-tuple-element.14, f32[4,12,64]{2,1,0:T(8,128)S(1)} %get-tuple-element.13), kind=kOutput, calls=%fused_computation.27 | convolution fusion | flops 456916992 | bytes 14954496 | tf_op jit(solution)/shard_map/nhqk,nkhd->nqhd/dot_general | solution.py:69
  359.3 0.5 copy.17
  359.8 0.5 reshape_reshape_reshape.7
  360.3 0.9 copy_bitcast_fusion.9
  (24 shorter events, 0.1 us)
Async XLA Ops:
  6.5 264.1 %copy-start = (s32[8,16]{1,0:T(8,128)S(1)}, s32[8,16]{1,0:T(8,128)}, u32[]{:S(2)}) copy-start(s32[8,16]{1,0:T(8,128)} %param.13) | copy-start | bytes 1540
  6.5 4.6 %copy-start.2 = (bf16[1,8,32,3072]{3,2,1,0:T(8,128)(2,1)S(1)}, bf16[1,8,32,3072]{3,2,1,0:T(8,128)(2,1)}, u32[]{:S(2)}) copy-start(bf16[1,8,32,3072]{3,2,1,0:T(8,128)(2,1)} %param.7) | copy-start | bytes 4718596
  6.5 4.6 %copy-start.6 = (f32[1,3072]{1,0:T(1,128)S(1)}, f32[1,3072]{1,0:T(1,128)}, u32[]{:S(2)}) copy-start(f32[1,3072]{1,0:T(1,128)} %param.9) | copy-start | bytes 36868
  6.5 4.6 %copy-start.5 = (f32[1,3072]{1,0:T(1,128)S(1)}, f32[1,3072]{1,0:T(1,128)}, u32[]{:S(2)}) copy-start(f32[1,3072]{1,0:T(1,128)} %param.8) | copy-start | bytes 36868
  6.5 167.6 %all-gather.2.cloned.1.call-start = ((), (), s32[]{:S(2)}) async-start(), calls=%async_computation | async-start | bytes 29196288 | tf_op jit(solution)/shard_map/all_gather | solution.py:82
  12.0 180.4 %copy-start.7 = (s32[1,4,9]{2,1,0:T(4,128)S(1)}, s32[1,4,9]{2,1,0:T(4,128)}, u32[]{:S(2)}) copy-start(s32[1,4,9]{2,1,0:T(4,128)} %param.11) | copy-start | bytes 436
  187.2 1.4 copy-start.4
  188.6 35.8 %collective-permute-start.1 = (bf16[8,32,3072]{2,1,0:T(8,128)(2,1)S(1)}, bf16[8,32,3072]{2,1,0:T(8,128)(2,1)S(1)}, u32[]{:S(2)}, u32[]{:S(2)}) collective-permute-start(bf16[8,32,3072]{2,1,0:T(8,128)(2,1)S(1)} %slice.31), channel_id=1, source_target_pairs={{32,0},{64,32},{96,64},{128,96},{160,128},{192,160},{224,192},{33,... | collective-permute-start | bytes 4718600 | tf_op jit(solution)/shard_map/ppermute | solution.py:22
  191.0 70.6 %collective-permute-start = (bf16[8,32,3072]{2,1,0:T(8,128)(2,1)S(1)}, bf16[8,32,3072]{2,1,0:T(8,128)(2,1)}, u32[]{:S(2)}, u32[]{:S(2)}) collective-permute-start(bf16[8,32,3072]{2,1,0:T(8,128)(2,1)S(1)} %slice.31), channel_id=1, source_target_pairs={{0,32},{32,64},{64,96},{96,128},{128,160},{160,192},{192,224},{1,3... | collective-permute-start | bytes 4718600 | tf_op jit(solution)/shard_map/ppermute | solution.py:21
  192.4 79.3 %copy-start.8 = (s32[1,4]{1,0:T(1,128)S(1)}, s32[1,4]{1,0:T(1,128)}, u32[]{:S(2)}) copy-start(s32[1,4]{1,0:T(1,128)} %param.12) | copy-start | bytes 52
  264.4 17.5 %collective-permute-start.2 = (bf16[24,8,3072]{2,1,0:T(8,128)(2,1)}, bf16[24,8,3072]{2,1,0:T(8,128)(2,1)}, u32[]{:S(2)}, u32[]{:S(2)}) collective-permute-start(bf16[24,8,3072]{2,1,0:T(8,128)(2,1)} %get-tuple-element.7), channel_id=1, source_target_pairs={{0,8},{8,16},{16,24},{1,9},{9,17},{17,25},{2,10},{10,18},{18,26},{... | collective-permute-start | bytes 3538952 | tf_op jit(solution)/shard_map/ppermute | solution.py:21
  268.5 17.8 %collective-permute-start.3 = (bf16[24,8,3072]{2,1,0:T(8,128)(2,1)}, bf16[24,8,3072]{2,1,0:T(8,128)(2,1)}, u32[]{:S(2)}, u32[]{:S(2)}) collective-permute-start(bf16[24,8,3072]{2,1,0:T(8,128)(2,1)} %get-tuple-element.8), channel_id=1, source_target_pairs={{8,0},{16,8},{24,16},{9,1},{17,9},{25,17},{10,2},{18,10},{26,18},{... | collective-permute-start | bytes 3538952 | tf_op jit(solution)/shard_map/ppermute | solution.py:22
  329.3 12.5 %copy-start.3 = (bf16[4,64,12,128]{3,2,1,0:T(8,128)(2,1)S(1)}, bf16[4,64,12,128]{3,2,1,0:T(8,128)(2,1)}, u32[]{:S(2)}) copy-start(bf16[4,64,12,128]{3,2,1,0:T(8,128)(2,1)} %reshape_reshape_reshape.6) | copy-start | bytes 2359300
  349.7 11.6 %copy-start.1 = (s32[8,16]{1,0:T(8,128)S(1)}, s32[8,16]{1,0:T(8,128)}, u32[]{:S(2)}) copy-start(s32[8,16]{1,0:T(8,128)} %param.13) | copy-start | bytes 1540
Sparse Core Ops, SparseCore 0:
  9.2 164.9 all-gather.1
where the time goes:
time: 369 us; the launch traced here: 368 us
  waiting for transfers between devices  242 us (66%)
  local copies, waits for them, and re-layouts  61.8 us (17%)
  matrix products  26 us (7%)
  other arithmetic  15.2 us (4%)
  between operations  13.6 us (4%)
  starting transfers between devices  9.95 us (3%)
    all_gather x1, waiting for transfers between devices, body(): lax.all_gather(qkv_weight, ('gx', 'wa'), axis=1, tiled=True)  162 us
    ppermute x2, waiting for transfers between devices, extended_2(): before = lax.ppermute(last, axis, up)  42.4 us
    ppermute x2, waiting for transfers between devices, extended_2(): after = lax.ppermute(first, axis, down)  36.3 us
    another operation x1, local copies, waits for them, and re-layouts, attend(): key_value = key_blocks.reshape(number, NBR * BLK * BLK, 2, HEADS, HD)  25.4 us
    dot_general x1, matrix products, body(): jnp.dot(flat_rows, lax.all_gather(qkv_weight, ('gx', 'wa'), axis=1, tiled...  13 us
    slice x1, local copies, waits for them, and re-layouts, attend(): key_value[:, :, 0]  12.5 us
    gather x1, local copies, waits for them, and re-layouts, body(): picked = key_blocks[row_ids + 1 + row_step, col_ids + 1 + col_step]  10.5 us
    dot_general x1, matrix products, attend(): jnp.einsum('nhqk,nkhd->nqhd', probs, key_value[:, :, 1], preferred_elemen...  9.59 us
  transfers between devices with their start and end apart: 5, of which 5 were waited for; matrix products, arithmetic and copies ran while one was open for 3% of the time, Pallas kernels for 0%

commit v1 on v0

--- a/solution.py
+++ b/solution.py
@@ -79,7 +79,12 @@
     flat_rows = normalize(tokens[0], mod_shift[0], mod_scale[0]).reshape(tile_rows * tile_cols, D)
     qkv = jnp.dot(
         flat_rows,
-        lax.all_gather(qkv_weight, ("gx", "wa"), axis=1, tiled=True),
+        jnp.concatenate(
+            lax.all_to_all(
+                jnp.stack([qkv_weight] * lax.axis_size(("gx", "wa"))), ("gx", "wa"), 0, 0
+            ),
+            axis=1,
+        ),
         preferred_element_type=jnp.float32,
     ).astype(jnp.bfloat16)
     qkv_grid = qkv.reshape(tile_rows, tile_cols, 3 * width)

time: 369 us -> 843 us (2.28)
  the two profiles are of different devices: /device:TPU:29 before, /device:TPU:105 now
where the time goes in v1:
time: 843 us; the launch traced here: 842 us
  waiting for transfers between devices  706 us (84%)
  local copies, waits for them, and re-layouts  72.1 us (9%)
  matrix products  26 us (3%)
  starting transfers between devices  25.3 us (3%)
  other arithmetic  12.5 us (1%)
    all_to_all x1, waiting for transfers between devices, body(): lax.all_to_all(jnp.stack([qkv_weight] * lax.axis_size(('gx', 'wa'))), ('g...  631 us
    ppermute x2, waiting for transfers between devices, extended_2(): after = lax.ppermute(first, axis, down)  38.3 us
    ppermute x2, waiting for transfers between devices, extended_2(): before = lax.ppermute(last, axis, up)  36 us
    another operation x1, local copies, waits for them, and re-layouts, attend(): key_value = key_blocks.reshape(number, NBR * BLK * BLK, 2, HEADS, HD)  25.4 us
  transfers between devices with their start and end apart: 5, of which 5 were waited for; matrix products, arithmetic and copies ran while one was open for 1% of the time, Pallas kernels for 0%

profile of v1, /device:TPU:105, one launch (start us, length us, event | category | flops | bytes accessed | tf_op | source)
XLA Modules:
  0.0 841.6 jit_solution(1359951872132075497)
XLA Ops:
  0.0 0.0 copy-start
  0.0 10.4 %stack.2 = bf16[32,3072,144]{1,2,0:T(8,128)(2,1)} broadcast(bf16[3072,144]{0,1:T(8,128)(2,1)} %param.10), dimensions={1,2} | broadcast | bytes 29196288 | tf_op jit(solution)/shard_map/stack | solution.py:84
  10.4 9.2 %all-to-all-start = ((bf16[32,3072,144]{1,2,0:T(8,128)(2,1)}), bf16[32,3072,144]{1,2,0:T(8,128)(2,1)}, u32[]{:S(2)}, u32[]{:S(2)}) async-start(bf16[32,3072,144]{1,2,0:T(8,128)(2,1)} %stack.2), calls=%async_computation | async-start | bytes 56623104 | tf_op jit(solution)/shard_map/all_to_all | solution.py:83
  19.6 0.0 copy-done.2
  19.6 0.3 convert_reduce_fusion
  19.9 0.6 fusion.13
  20.5 0.0 copy-done.6
  20.5 0.8 fusion.10
  21.3 631.2 %all-to-all-done = bf16[32,3072,144]{1,2,0:T(8,128)(2,1)} async-done(((bf16[32,3072,144]{1,2,0:T(8,128)(2,1)}), bf16[32,3072,144]{1,2,0:T(8,128)(2,1)}, u32[]{:S(2)}, u32[]{:S(2)}) %all-to-all-start) | async-done | bytes 28311584 | tf_op jit(solution)/shard_map/all_to_all | solution.py:83
  652.5 13.0 %convolution_convert_fusion = bf16[256,4608]{1,0:T(8,128)(2,1)S(1)} fusion(bf16[256,3072]{1,0:T(8,128)(2,1)S(1)} %bitcast.67, bf16[3072,4608]{0,1:T(8,128)(2,1)} %bitcast.5), kind=kOutput, calls=%fused_computation.12 | convolution fusion | flops 7248936960 | bytes 32243712 | tf_op jit(solution)/shard_map/dot_general | solution.py:80
  665.6 0.2 slice.31
  665.8 1.2 copy-done.4
  667.0 4.3 collective-permute-start
  671.4 3.3 collective-permute-start.1
  674.7 0.1 fusion.20
  674.8 0.0 copy-start.8
  674.8 30.9 %collective-permute-done = bf16[8,32,3072]{2,1,0:T(8,128)(2,1)S(1)} collective-permute-done((bf16[8,32,3072]{2,1,0:T(8,128)(2,1)S(1)}, bf16[8,32,3072]{2,1,0:T(8,128)(2,1)S(1)}, u32[]{:S(2)}, u32[]{:S(2)}) %collective-permute-start) | collective-permute-done | bytes 1572896 | tf_op jit(solution)/shard_map/ppermute | solution.py:21
  705.7 33.9 %collective-permute-done.1 = bf16[8,32,3072]{2,1,0:T(8,128)(2,1)} collective-permute-done((bf16[8,32,3072]{2,1,0:T(8,128)(2,1)S(1)}, bf16[8,32,3072]{2,1,0:T(8,128)(2,1)}, u32[]{:S(2)}, u32[]{:S(2)}) %collective-permute-start.1) | collective-permute-done | bytes 1572896 | tf_op jit(solution)/shard_map/ppermute | solution.py:22
  739.6 2.9 pad_maximum_fusion.3
  742.5 6.3 collective-permute-start.2
  748.8 2.1 collective-permute-start.3
  750.9 0.1 reshape.155
  751.0 0.1 reshape.163
  751.1 0.9 gather_fusion.1
  751.9 0.1 lt.77
  752.0 0.1 lt.78
  752.1 0.1 lt.79
  752.2 0.1 lt.73
  752.3 0.1 iota_compare_fusion
  752.3 0.1 and.28
  752.4 0.1 and.29
  752.5 1.2 slice_bitcast_fusion
  753.7 0.9 copy.15
  754.7 2.4 reshape_reshape_reshape.6
  757.0 5.2 collective-permute-done.2
  762.2 4.4 collective-permute-done.3
  766.6 3.3 pad_maximum_fusion
  769.9 3.7 copy.34
  773.6 10.6 %gather_fusion = bf16[36,64,3072]{2,1,0:T(8,128)(2,1)} fusion(bf16[3,6,64,3072]{3,2,1,0:T(8,128)(2,1)} %bitcast.63, s32[36]{0:T(128)S(1)} %reshape.155), kind=kCustom, calls=%fused_computation | custom fusion | bytes 28311840 | tf_op jit(solution)/shard_map/gather | solution.py:100
  784.2 25.4 %reshape_reshape.3 = bf16[4,576,2,12,128]{4,3,2,1,0:T(8,128)(2,1)} reshape(bf16[36,64,3072]{2,1,0:T(8,128)(2,1)} %gather_fusion) | data formatting | bytes 28311552 | tf_op jit(solution)/shard_map/reshape;reshape | solution.py:61
  809.6 12.5 %fusion.31 = (bf16[4,576,1,12,128]{4,3,2,1,0:T(8,128)(2,1)S(1)}, bf16[4,576,1,12,128]{4,3,2,1,0:T(8,128)(2,1)}) fusion(bf16[4,576,2,12,128]{4,3,2,1,0:T(8,128)(2,1)} %reshape_reshape.3), kind=kLoop, calls=%fused_computation.70 | loop fusion | bytes 28311552 | tf_op jit(solution)/shard_map/slice | solution.py:63
  822.2 3.4 fusion.2
  825.6 4.4 fusion.32
  830.0 9.6 %fusion.15 = bf16[4,64,12,128]{3,1,2,0:T(8,128)(2,1)S(1)} fusion(bf16[4,576,1,12,128]{4,3,2,1,0:T(8,128)(2,1)} %get-tuple-element.6, f32[4,12,64,576]{3,2,1,0:T(8,128)} %get-tuple-element.14, f32[4,12,64]{2,1,0:T(8,128)S(1)} %get-tuple-element.13), kind=kOutput, calls=%fused_computation.28 | convolution fusion | flops 456916992 | bytes 14954496 | tf_op jit(solution)/shard_map/nhqk,nkhd->nqhd/dot_general | solution.py:69
  839.6 0.5 copy.18
  840.1 0.5 reshape_reshape_reshape.7
  840.7 0.9 copy_bitcast_fusion.9
  841.6 0.0 copy-done.1
  (22 shorter events, 0.1 us)
Async XLA Ops:
  0.0 751.1 %copy-start = (s32[8,16]{1,0:T(8,128)S(1)}, s32[8,16]{1,0:T(8,128)}, u32[]{:S(2)}) copy-start(s32[8,16]{1,0:T(8,128)} %param.13) | copy-start | bytes 1540
  10.4 9.2 %copy-start.2 = (bf16[1,8,32,3072]{3,2,1,0:T(8,128)(2,1)S(1)}, bf16[1,8,32,3072]{3,2,1,0:T(8,128)(2,1)}, u32[]{:S(2)}) copy-start(bf16[1,8,32,3072]{3,2,1,0:T(8,128)(2,1)} %param.7) | copy-start | bytes 4718596
  10.4 10.1 %copy-start.6 = (f32[1,3072]{1,0:T(1,128)S(1)}, f32[1,3072]{1,0:T(1,128)}, u32[]{:S(2)}) copy-start(f32[1,3072]{1,0:T(1,128)} %param.9) | copy-start | bytes 36868
  10.4 10.1 %copy-start.5 = (f32[1,3072]{1,0:T(1,128)S(1)}, f32[1,3072]{1,0:T(1,128)}, u32[]{:S(2)}) copy-start(f32[1,3072]{1,0:T(1,128)} %param.8) | copy-start | bytes 36868
  10.4 642.1 %all-to-all-start = ((bf16[32,3072,144]{1,2,0:T(8,128)(2,1)}), bf16[32,3072,144]{1,2,0:T(8,128)(2,1)}, u32[]{:S(2)}, u32[]{:S(2)}) async-start(bf16[32,3072,144]{1,2,0:T(8,128)(2,1)} %stack.2), calls=%async_computation | async-start | bytes 56623104 | tf_op jit(solution)/shard_map/all_to_all | solution.py:83
  652.5 22.2 %copy-start.7 = (s32[1,4,9]{2,1,0:T(4,128)S(1)}, s32[1,4,9]{2,1,0:T(4,128)}, u32[]{:S(2)}) copy-start(s32[1,4,9]{2,1,0:T(4,128)} %param.11) | copy-start | bytes 436
  665.6 1.4 copy-start.4
  667.0 38.7 %collective-permute-start = (bf16[8,32,3072]{2,1,0:T(8,128)(2,1)S(1)}, bf16[8,32,3072]{2,1,0:T(8,128)(2,1)S(1)}, u32[]{:S(2)}, u32[]{:S(2)}) collective-permute-start(bf16[8,32,3072]{2,1,0:T(8,128)(2,1)S(1)} %slice.31), channel_id=1, source_target_pairs={{0,32},{32,64},{64,96},{96,128},{128,160},{160,192},{192,224},{1,3... | collective-permute-start | bytes 4718600 | tf_op jit(solution)/shard_map/ppermute | solution.py:21
  671.4 68.3 %collective-permute-start.1 = (bf16[8,32,3072]{2,1,0:T(8,128)(2,1)S(1)}, bf16[8,32,3072]{2,1,0:T(8,128)(2,1)}, u32[]{:S(2)}, u32[]{:S(2)}) collective-permute-start(bf16[8,32,3072]{2,1,0:T(8,128)(2,1)S(1)} %slice.31), channel_id=1, source_target_pairs={{32,0},{64,32},{96,64},{128,96},{160,128},{192,160},{224,192},{33,... | collective-permute-start | bytes 4718600 | tf_op jit(solution)/shard_map/ppermute | solution.py:22
  674.8 77.4 %copy-start.8 = (s32[1,4]{1,0:T(1,128)S(1)}, s32[1,4]{1,0:T(1,128)}, u32[]{:S(2)}) copy-start(s32[1,4]{1,0:T(1,128)} %param.12) | copy-start | bytes 52
  742.5 19.7 %collective-permute-start.2 = (bf16[24,8,3072]{2,1,0:T(8,128)(2,1)}, bf16[24,8,3072]{2,1,0:T(8,128)(2,1)}, u32[]{:S(2)}, u32[]{:S(2)}) collective-permute-start(bf16[24,8,3072]{2,1,0:T(8,128)(2,1)} %get-tuple-element.7), channel_id=1, source_target_pairs={{0,8},{8,16},{16,24},{1,9},{9,17},{17,25},{2,10},{10,18},{18,26},{... | collective-permute-start | bytes 3538952 | tf_op jit(solution)/shard_map/ppermute | solution.py:21
  748.8 17.8 %collective-permute-start.3 = (bf16[24,8,3072]{2,1,0:T(8,128)(2,1)}, bf16[24,8,3072]{2,1,0:T(8,128)(2,1)}, u32[]{:S(2)}, u32[]{:S(2)}) collective-permute-start(bf16[24,8,3072]{2,1,0:T(8,128)(2,1)} %get-tuple-element.8), channel_id=1, source_target_pairs={{8,0},{16,8},{24,16},{9,1},{17,9},{25,17},{10,2},{18,10},{26,18},{... | collective-permute-start | bytes 3538952 | tf_op jit(solution)/shard_map/ppermute | solution.py:22
  809.6 12.5 %copy-start.3 = (bf16[4,64,12,128]{3,2,1,0:T(8,128)(2,1)S(1)}, bf16[4,64,12,128]{3,2,1,0:T(8,128)(2,1)}, u32[]{:S(2)}) copy-start(bf16[4,64,12,128]{3,2,1,0:T(8,128)(2,1)} %reshape_reshape_reshape.6) | copy-start | bytes 2359300
  830.0 11.6 %copy-start.1 = (s32[8,16]{1,0:T(8,128)S(1)}, s32[8,16]{1,0:T(8,128)}, u32[]{:S(2)}) copy-start(s32[8,16]{1,0:T(8,128)} %param.13) | copy-start | bytes 1540
